TPU v7x, 32 devices: a whole 2x2x4 slice. The times are simulated.
32 devices in a mesh: gx: 4 (over z), gy: 4 (over y, x), gz: 2 (over core).
Axes of the slice: x: 2, y: 2, z: 4, core: 2. Of those that a mesh axis runs over, the one named last changes fastest.
Arguments:
- residual: float32 [128, 139264], P(None, ('gx', 'gy', 'gz')), may hold values from -6 to 6
- diag_inverse: bfloat16 [640, 256, 256], P(('gx', 'gy', 'gz'))
- coupling: bfloat16 [608, 256, 256], P(('gx', 'gy', 'gz')), may hold values from -0.09375 to 0.09375
- parent: int32 [640], P(('gx', 'gy', 'gz')), may hold values from 0 to 18, as said below
- send_rows: int32 [192, 128], P(('gx', 'gy', 'gz')), may hold values from 0 to 4351
- counts: int32 [32], P(('gx', 'gy', 'gz')), may hold values from 10 to 40, as said below
- deflation: float32 [40, 139264], P(None, ('gx', 'gy', 'gz')), may hold values from -0.09375 to 0.09375
- coarse_inverse: float32 [1280, 1280], P(('gx', 'gy', 'gz')), as said below
Outputs:
- preconditioned: float32 [128, 139264], P(None, ('gx', 'gy', 'gz'))
Inputs may be any that keep to these rules, and one draw needn't show every extreme that they name: The parent of supernode b >= 1 is one of b - 4 to b - 1 of the same subdomain (0 at the least), the last supernode's parent is the one before it, and the entry of supernode 0 is 0. `counts`: every draw has a subdomain with 40 and one with 10 vectors. coarse_inverse is symmetric.
All inputs are finite; a program needn't handle non-finite values.
Results may differ from a plain program's by a relative error of at most 0.005.
Values may be sent and summed in bfloat16 or wider, within the bound.
No kernel may reach another device: no remote copies, remote signals or barrier semaphores. Data moves between devices by JAX's collectives and lax.ppermute only.
A program may use at most 128 MiB of HBM per device.

v0:
```python
import jax
import jax.numpy as jnp
from jax import lax
from jax.sharding import PartitionSpec as P


def with_halo(block, sides, width):
    for axis, dim in sides:
        count = lax.axis_size(axis)
        forward = [(i, i + 1) for i in range(count - 1)]
        backward = [(target, source) for source, target in forward]
        low = lax.ppermute(
            lax.slice_in_dim(block, block.shape[dim] - width, None, axis=dim), axis, forward
        )
        high = lax.ppermute(lax.slice_in_dim(block, 0, width, axis=dim), axis, backward)
        block = jnp.concatenate([low, block, high], axis=dim)
    return block


def solve_local(extended, diag_inverse, coupling, parent):
    nrhs_here, width_ext = extended.shape
    blocks_n, block_w, _ = diag_inverse.shape
    blocks = extended.reshape(nrhs_here, blocks_n, block_w).transpose(1, 0, 2)
    first = jnp.einsum(
        "rs,ts->rt",
        blocks[0].astype(jnp.bfloat16),
        diag_inverse[0],
        preferred_element_type=jnp.float32,
    ).astype(jnp.bfloat16)
    store = jnp.zeros((blocks_n, nrhs_here, block_w), jnp.bfloat16).at[0].set(first)
    places = lax.iota(jnp.int32, blocks_n)

    def forward(store, item):
        block, inverse_blk, couple, link, place = item
        prior = lax.dynamic_index_in_dim(store, link, 0, keepdims=False)
        lower = (
            block - jnp.einsum("rs,ts->rt", prior, couple, preferred_element_type=jnp.float32)
        ).astype(jnp.bfloat16)
        value = jnp.einsum(
            "rs,ts->rt", lower, inverse_blk, preferred_element_type=jnp.float32
        ).astype(jnp.bfloat16)
        return (lax.dynamic_update_index_in_dim(store, value, place, 0), None)

    store, _ = lax.scan(
        forward, store, (blocks[1:], diag_inverse[1:], coupling, parent[1:], places[1:])
    )

    def backward(carry, item):
        value, inverse_blk, link, place = item
        upper = (
            value.astype(jnp.float32) - lax.dynamic_index_in_dim(carry, place, 0, keepdims=False)
        ).astype(jnp.bfloat16)
        result = jnp.einsum(
            "rs,st->rt", upper, inverse_blk, preferred_element_type=jnp.float32
        ).astype(jnp.bfloat16)
        couple = lax.dynamic_index_in_dim(coupling, jnp.maximum(place - 1, 0), 0, keepdims=False)
        push = jnp.einsum("rs,st->rt", result, couple, preferred_element_type=jnp.float32) * (
            place > 0
        ).astype(jnp.float32)
        target = lax.dynamic_index_in_dim(carry, link, 0, keepdims=False)
        carry = lax.dynamic_update_index_in_dim(carry, target + push, link, 0)
        return (carry, result)

    empty = jnp.zeros((blocks_n, nrhs_here, block_w), jnp.float32)
    _, solved = lax.scan(backward, empty, (store, diag_inverse, parent, places), reverse=True)
    return solved.transpose(1, 0, 2).reshape(nrhs_here, width_ext)


def pick_slot(padded, axis_pos, coord, slot_id):
    where_at = [1, 1, 1]
    where_at[axis_pos] = coord
    return padded[where_at[0], where_at[1], where_at[2], slot_id]


def per_device(
    residual, diag_inverse, coupling, parent, send_rows, counts, deflation, coarse_inverse
):
    nrhs_here, owned_n = residual.shape
    slots_n, face_w = send_rows.shape
    kmax_here = deflation.shape[0]
    outgoing = jnp.moveaxis(jnp.take(residual, send_rows, axis=1), 1, 0)
    mask = (lax.iota(jnp.int32, kmax_here) < counts[0]).astype(jnp.float32)
    vectors = deflation * mask[:, None]
    coeffs = jnp.dot(
        residual, vectors.T, precision=lax.Precision.HIGHEST, preferred_element_type=jnp.float32
    )
    padded = with_halo(outgoing[None, None, None], (("gx", 0), ("gy", 1), ("gz", 2)), 1)
    incoming = []
    for axis_pos in range(3):
        incoming.append(pick_slot(padded, axis_pos, 2, 2 * axis_pos))
        incoming.append(pick_slot(padded, axis_pos, 0, 2 * axis_pos + 1))
    extended = jnp.concatenate([residual] + incoming, axis=1)
    solved = solve_local(extended, diag_inverse, coupling, parent)
    corrections = jnp.moveaxis(solved[:, owned_n:].reshape(nrhs_here, slots_n, face_w), 1, 0)
    back = with_halo(corrections[None, None, None], (("gx", 0), ("gy", 1), ("gz", 2)), 1)
    returned = []
    for axis_pos in range(3):
        returned.append(pick_slot(back, axis_pos, 0, 2 * axis_pos))
        returned.append(pick_slot(back, axis_pos, 2, 2 * axis_pos + 1))
    solved_coarse = lax.dot_general(
        lax.all_gather(coeffs, ("gx", "gy", "gz"), axis=1, tiled=True),
        coarse_inverse,
        (((1,), (1,)), ((), ())),
        precision=lax.Precision.HIGHEST,
        preferred_element_type=jnp.float32,
    )
    total = solved[:, :owned_n].astype(jnp.float32)
    for slot_id in range(6):
        total = total.at[:, send_rows[slot_id]].add(returned[slot_id].astype(jnp.float32))
    total = total + jnp.dot(
        solved_coarse, vectors, precision=lax.Precision.HIGHEST, preferred_element_type=jnp.float32
    )
    return total


def solution(mesh):
    return jax.shard_map(
        per_device,
        mesh=mesh,
        in_specs=(
            P(None, ("gx", "gy", "gz")),
            P(("gx", "gy", "gz"), None, None),
            P(("gx", "gy", "gz"), None, None),
            P(("gx", "gy", "gz")),
            P(("gx", "gy", "gz"), None),
            P(("gx", "gy", "gz")),
            P(None, ("gx", "gy", "gz")),
            P(("gx", "gy", "gz"), None),
        ),
        out_specs=P(None, ("gx", "gy", "gz")),
        check_vma=False,
    )
```

profile of v0, /device:TPU:0, one launch (start us, length us, event | category | flops | bytes accessed | tf_op | source)
XLA Modules:
  0.0 555.2 jit_solution(16365458862300856485)
XLA Ops:
  1.4 2.0 copy.16
  6.5 5.6 %collective-permute-start.1 = (f32[1,1,1,6,128,128]{4,5,3,2,1,0:T(8,128)S(1)}, f32[1,1,1,6,128,128]{4,5,3,2,1,0:T(8,128)S(1)}, u32[]{:S(2)}, u32[]{:S(2)}) collective-permute-start(f32[1,1,1,6,128,128]{4,5,3,2,1,0:T(8,128)S(1)} %select_bitcast_fusion), channel_id=1, source_target_pairs={{0,8},{8,16},{16,24},{1,9},{9,17},{17,25},{2,10},{10,18},{18,26},{... | collective-permute-start | bytes 1179656 | tf_op jit(solution)/shard_map/ppermute | solution.py:12
  12.1 7.2 %collective-permute-done = f32[1,1,1,6,128,128]{4,5,3,2,1,0:T(8,128)S(1)} collective-permute-done((f32[1,1,1,6,128,128]{4,5,3,2,1,0:T(8,128)S(1)}, f32[1,1,1,6,128,128]{4,5,3,2,1,0:T(8,128)S(1)}, u32[]{:S(2)}, u32[]{:S(2)}) %collective-permute-start) | collective-permute-done | bytes 393248 | tf_op jit(solution)/shard_map/ppermute | solution.py:15
  21.8 4.6 collective-permute-start.3
  26.5 24.9 %collective-permute-done.2 = f32[3,1,1,6,128,128]{4,5,3,2,1,0:T(8,128)S(1)} collective-permute-done((f32[3,1,1,6,128,128]{4,5,3,2,1,0:T(8,128)S(1)}, f32[3,1,1,6,128,128]{4,5,3,2,1,0:T(8,128)S(1)}, u32[]{:S(2)}, u32[]{:S(2)}) %collective-permute-start.2) | collective-permute-done | bytes 1179680 | tf_op jit(solution)/shard_map/ppermute | solution.py:15
  51.3 2.1 pad_maximum_fusion
  55.2 6.7 %collective-permute-start.5 = (f32[3,3,1,6,128,128]{4,5,3,2,1,0:T(8,128)}, f32[3,3,1,6,128,128]{4,5,3,2,1,0:T(8,128)}, u32[]{:S(2)}, u32[]{:S(2)}) collective-permute-start(f32[3,3,1,6,128,128]{4,5,3,2,1,0:T(8,128)} %pad_maximum_fusion), channel_id=1, source_target_pairs={{0,1},{2,3},{4,5},{6,7},{8,9},{10,11},{12,13},{14,15},{16,17},{18,... | collective-permute-start | bytes 10616840 | tf_op jit(solution)/shard_map/ppermute | solution.py:12
  61.8 3.4 slice.108
  71.5 148.3 %while.28 = (s32[]{:T(128)}, bf16[20,128,256]{2,1,0:T(8,128)(2,1)}, f32[19,128,256]{1,2,0:T(8,128)S(1)}, s32[19]{0:T(128)S(1)}, bf16[19,256,256]{2,1,0:T(8,128)(...) while((s32[]{:T(128)}, bf16[20,128,256]{2,1,0:T(8,128)(2,1)}, ...), condition=%wide.region_1.2_spmd, body=%wide.region_0.1_spmd.sunk | while | flops 33652744 | bytes 1180877 | solution.py:44
  77.3 1.9 fusion.72
  85.1 1.9 fusion.72
  92.9 1.9 fusion.72
  100.7 1.9 fusion.72
  108.5 1.9 fusion.72
  116.3 1.9 fusion.72
  124.1 1.9 fusion.72
  131.9 1.9 fusion.72
  139.7 1.9 fusion.72
  147.6 1.9 fusion.72
  155.4 1.9 fusion.72
  163.2 1.9 fusion.72
  171.0 1.9 fusion.72
  178.8 1.9 fusion.72
  186.6 1.9 fusion.72
  194.4 1.9 fusion.72
  202.2 1.9 fusion.72
  210.0 1.9 fusion.72
  217.8 1.9 fusion.72
  221.4 183.8 %while.29 = (s32[]{:T(128)}, f32[20,128,256]{2,1,0:T(8,128)S(1)}, bf16[20,128,256]{1,2,0:T(8,128)(2,1)}, s32[20]{0:T(128)S(1)}, bf16[20,128,256]{2,1,0:T(8,128)(...) while((s32[]{:T(128)}, f32[20,128,256]{2,1,0:T(8,128)S(1)}, ...), condition=%wide.region_3.4_spmd, body=%wide.region_2.3_spmd.sunk | while | flops 33751048 | bytes 1378079 | solution.py:65
  406.1 4.7 collective-permute-start.6
  412.1 1.9 collective-permute-done.6
  414.0 4.4 collective-permute-done.7
  418.4 24.2 %collective-permute-start.8 = (bf16[3,1,1,6,128,128]{4,5,3,2,1,0:T(8,128)(2,1)S(1)}, bf16[3,1,1,6,128,128]{4,5,3,2,1,0:T(8,128)(2,1)S(1)}, u32[]{:S(2)}, u32[]{:S(2)}) collective-permute-start(bf16[3,1,1,6,128,128]{4,5,3,2,1,0:T(8,128)(2,1)S(1)} %pad_maximum_fusion.3), channel_id=1, source_target_pairs={{0,2},{2,4},{4,6},{1,3},{3,5},{5,7},{8,10},{10,12},{12,14},{9,11},... | collective-permute-start | bytes 1769480 | tf_op jit(solution)/shard_map/ppermute | solution.py:12
  444.0 8.4 %collective-permute-done.8 = bf16[3,1,1,6,128,128]{4,5,3,2,1,0:T(8,128)(2,1)S(1)} collective-permute-done((bf16[3,1,1,6,128,128]{4,5,3,2,1,0:T(8,128)(2,1)S(1)}, bf16[3,1,1,6,128,128]{4,5,3,2,1,0:T(8,128)(2,1)S(1)}, u32[]{:S(2)}, u32[]{:S(2)}) %collective-permute-start.8) | collective-permute-done | bytes 589856 | tf_op jit(solution)/shard_map/ppermute | solution.py:12
  452.4 16.5 %collective-permute-done.9 = bf16[3,1,1,6,128,128]{4,5,3,2,1,0:T(8,128)(2,1)S(1)} collective-permute-done((bf16[3,1,1,6,128,128]{4,5,3,2,1,0:T(8,128)(2,1)S(1)}, bf16[3,1,1,6,128,128]{4,5,3,2,1,0:T(8,128)(2,1)S(1)}, u32[]{:S(2)}, u32[]{:S(2)}) %collective-permute-start.9) | collective-permute-done | bytes 589856 | tf_op jit(solution)/shard_map/ppermute | solution.py:15
  470.3 2.5 collective-permute-start.10
  475.4 2.4 convolution_bitcast_fusion
  477.8 40.4 %all_gather.3 = f32[128,1280]{0,1:T(8,128)S(1)} all-gather(f32[128,40]{0,1:T(8,128)S(1)} %convolution_bitcast_fusion), channel_id=1, replica_groups=mesh['gx'=4,'gy'=4,'gz'=2] {'gx','gy','gz'}, dimensions={1}, use_global_device_ids=true | all-gather | bytes 675840 | tf_op jit(solution)/shard_map/all_gather | solution.py:101
  518.2 1.8 fusion.54
  520.8 3.1 convolution_add_fusion
  524.0 1.9 copy.20
  525.9 4.4 scatter_custom_fusion
  530.3 4.4 scatter_custom_fusion.1
  534.7 4.4 scatter_custom_fusion.2
  539.1 4.4 scatter_custom_fusion.3
  543.5 4.4 scatter_custom_fusion.4
  547.9 4.4 scatter_custom_fusion.5
  552.2 3.0 copy.21
  (300 shorter events, 149.7 us)
Async XLA Ops:
  0.0 518.2 %copy-start = (f32[40,1280]{1,0:T(8,128)S(1)}, f32[40,1280]{1,0:T(8,128)}, u32[]{:S(2)}) copy-start(f32[40,1280]{1,0:T(8,128)} %param.21) | copy-start | bytes 614404
  5.2 14.0 %collective-permute-start = (f32[1,1,1,6,128,128]{4,5,3,2,1,0:T(8,128)S(1)}, f32[1,1,1,6,128,128]{4,5,3,2,1,0:T(8,128)S(1)}, u32[]{:S(2)}, u32[]{:S(2)}) collective-permute-start(f32[1,1,1,6,128,128]{4,5,3,2,1,0:T(8,128)S(1)} %select_bitcast_fusion), channel_id=1, source_target_pairs={{8,0},{16,8},{24,16},{9,1},{17,9},{25,17},{10,2},{18,10},{26,18},{... | collective-permute-start | bytes 1179656 | tf_op jit(solution)/shard_map/ppermute | solution.py:15
  6.5 13.9 %collective-permute-start.1 = (f32[1,1,1,6,128,128]{4,5,3,2,1,0:T(8,128)S(1)}, f32[1,1,1,6,128,128]{4,5,3,2,1,0:T(8,128)S(1)}, u32[]{:S(2)}, u32[]{:S(2)}) collective-permute-start(f32[1,1,1,6,128,128]{4,5,3,2,1,0:T(8,128)S(1)} %select_bitcast_fusion), channel_id=1, source_target_pairs={{0,8},{8,16},{16,24},{1,9},{9,17},{17,25},{2,10},{10,18},{18,26},{... | collective-permute-start | bytes 1179656 | tf_op jit(solution)/shard_map/ppermute | solution.py:12
  20.5 30.8 %collective-permute-start.2 = (f32[3,1,1,6,128,128]{4,5,3,2,1,0:T(8,128)S(1)}, f32[3,1,1,6,128,128]{4,5,3,2,1,0:T(8,128)S(1)}, u32[]{:S(2)}, u32[]{:S(2)}) collective-permute-start(f32[3,1,1,6,128,128]{4,5,3,2,1,0:T(8,128)S(1)} %pad_maximum_fusion.2), channel_id=1, source_target_pairs={{2,0},{4,2},{6,4},{3,1},{5,3},{7,5},{10,8},{12,10},{14,12},{11,9},... | collective-permute-start | bytes 3538952 | tf_op jit(solution)/shard_map/ppermute | solution.py:15
  21.8 29.5 %collective-permute-start.3 = (f32[3,1,1,6,128,128]{4,5,3,2,1,0:T(8,128)S(1)}, f32[3,1,1,6,128,128]{4,5,3,2,1,0:T(8,128)S(1)}, u32[]{:S(2)}, u32[]{:S(2)}) collective-permute-start(f32[3,1,1,6,128,128]{4,5,3,2,1,0:T(8,128)S(1)} %pad_maximum_fusion.2), channel_id=1, source_target_pairs={{0,2},{2,4},{4,6},{1,3},{3,5},{5,7},{8,10},{10,12},{12,14},{9,11},... | collective-permute-start | bytes 3538952 | tf_op jit(solution)/shard_map/ppermute | solution.py:12
  51.3 2.2 copy-start.4
  51.3 2.6 copy-start.5
  53.9 13.4 %collective-permute-start.4 = (f32[3,3,1,6,128,128]{4,5,3,2,1,0:T(8,128)}, f32[3,3,1,6,128,128]{4,5,3,2,1,0:T(8,128)}, u32[]{:S(2)}, u32[]{:S(2)}) collective-permute-start(f32[3,3,1,6,128,128]{4,5,3,2,1,0:T(8,128)} %pad_maximum_fusion), channel_id=1, source_target_pairs={{1,0},{3,2},{5,4},{7,6},{9,8},{11,10},{13,12},{15,14},{17,16},{19,... | collective-permute-start | bytes 10616840 | tf_op jit(solution)/shard_map/ppermute | solution.py:15
  55.2 13.0 %collective-permute-start.5 = (f32[3,3,1,6,128,128]{4,5,3,2,1,0:T(8,128)}, f32[3,3,1,6,128,128]{4,5,3,2,1,0:T(8,128)}, u32[]{:S(2)}, u32[]{:S(2)}) collective-permute-start(f32[3,3,1,6,128,128]{4,5,3,2,1,0:T(8,128)} %pad_maximum_fusion), channel_id=1, source_target_pairs={{0,1},{2,3},{4,5},{6,7},{8,9},{10,11},{12,13},{14,15},{16,17},{18,... | collective-permute-start | bytes 10616840 | tf_op jit(solution)/shard_map/ppermute | solution.py:12
  61.8 3.5 copy-start.11
  406.1 68.7 %copy-start.10 = (s32[6,128]{1,0:T(8,128)S(1)}, s32[6,128]{1,0:T(8,128)}, u32[]{:S(2)}) copy-start(s32[6,128]{1,0:T(8,128)} %param.18) | copy-start | bytes 9220
  406.1 69.3 %copy-start.1 = (f32[128,4352]{1,0:T(8,128)S(1)}, f32[128,4352]{1,0:T(8,128)}, u32[]{:S(2)}) copy-start(f32[128,4352]{1,0:T(8,128)} %param.14) | copy-start | bytes 6684676
  406.1 69.3 %copy-start.3 = (f32[40,4352]{1,0:T(8,128)S(1)}, f32[40,4352]{1,0:T(8,128)}, u32[]{:S(2)}) copy-start(f32[40,4352]{1,0:T(8,128)} %param.20) | copy-start | bytes 2088964
  406.1 7.8 %collective-permute-start.6 = (bf16[1,1,1,6,128,128]{4,5,3,2,1,0:T(8,128)(2,1)S(1)}, bf16[1,1,1,6,128,128]{4,5,3,2,1,0:T(8,128)(2,1)S(1)}, u32[]{:S(2)}, u32[]{:S(2)}) collective-permute-start(bf16[1,1,1,6,128,128]{4,5,3,2,1,0:T(8,128)(2,1)S(1)} %bitcast.215), channel_id=1, source_target_pairs={{0,8},{8,16},{16,24},{1,9},{9,17},{17,25},{2,10},{10,18},{18,26},{... | collective-permute-start | bytes 589832 | tf_op jit(solution)/shard_map/ppermute | solution.py:12
  410.8 7.6 %collective-permute-start.7 = (bf16[1,1,1,6,128,128]{4,5,3,2,1,0:T(8,128)(2,1)S(1)}, bf16[1,1,1,6,128,128]{4,5,3,2,1,0:T(8,128)(2,1)S(1)}, u32[]{:S(2)}, u32[]{:S(2)}) collective-permute-start(bf16[1,1,1,6,128,128]{4,5,3,2,1,0:T(8,128)(2,1)S(1)} %bitcast.216), channel_id=1, source_target_pairs={{8,0},{16,8},{24,16},{9,1},{17,9},{25,17},{10,2},{18,10},{26,18},{... | collective-permute-start | bytes 589832 | tf_op jit(solution)/shard_map/ppermute | solution.py:15
  414.0 56.3 %copy-start.6 = (bf16[1,1,1,6,128,128]{4,5,3,2,1,0:T(8,128)(2,1)}, bf16[1,1,1,6,128,128]{4,5,3,2,1,0:T(8,128)(2,1)S(1)}, u32[]{:S(2)}) copy-start(bf16[1,1,1,6,128,128]{4,5,3,2,1,0:T(8,128)(2,1)S(1)} %collective-permute-done.6) | copy-start | bytes 589828
  418.4 51.9 %copy-start.7 = (bf16[1,1,1,6,128,128]{4,5,3,2,1,0:T(8,128)(2,1)}, bf16[1,1,1,6,128,128]{4,5,3,2,1,0:T(8,128)(2,1)S(1)}, u32[]{:S(2)}) copy-start(bf16[1,1,1,6,128,128]{4,5,3,2,1,0:T(8,128)(2,1)S(1)} %collective-permute-done.7) | copy-start | bytes 589828
  418.4 34.0 %collective-permute-start.8 = (bf16[3,1,1,6,128,128]{4,5,3,2,1,0:T(8,128)(2,1)S(1)}, bf16[3,1,1,6,128,128]{4,5,3,2,1,0:T(8,128)(2,1)S(1)}, u32[]{:S(2)}, u32[]{:S(2)}) collective-permute-start(bf16[3,1,1,6,128,128]{4,5,3,2,1,0:T(8,128)(2,1)S(1)} %pad_maximum_fusion.3), channel_id=1, source_target_pairs={{0,2},{2,4},{4,6},{1,3},{3,5},{5,7},{8,10},{10,12},{12,14},{9,11},... | collective-permute-start | bytes 1769480 | tf_op jit(solution)/shard_map/ppermute | solution.py:12
  442.7 26.2 %collective-permute-start.9 = (bf16[3,1,1,6,128,128]{4,5,3,2,1,0:T(8,128)(2,1)S(1)}, bf16[3,1,1,6,128,128]{4,5,3,2,1,0:T(8,128)(2,1)S(1)}, u32[]{:S(2)}, u32[]{:S(2)}) collective-permute-start(bf16[3,1,1,6,128,128]{4,5,3,2,1,0:T(8,128)(2,1)S(1)} %pad_maximum_fusion.3), channel_id=1, source_target_pairs={{2,0},{4,2},{6,4},{3,1},{5,3},{7,5},{10,8},{12,10},{14,12},{11,9},... | collective-permute-start | bytes 1769480 | tf_op jit(solution)/shard_map/ppermute | solution.py:15
  452.4 25.4 %copy-start.8 = (bf16[3,1,1,6,128,128]{4,5,3,2,1,0:T(8,128)(2,1)}, bf16[3,1,1,6,128,128]{4,5,3,2,1,0:T(8,128)(2,1)S(1)}, u32[]{:S(2)}) copy-start(bf16[3,1,1,6,128,128]{4,5,3,2,1,0:T(8,128)(2,1)S(1)} %collective-permute-done.8) | copy-start | bytes 1769476
  468.9 8.9 %copy-start.9 = (bf16[3,1,1,6,128,128]{4,5,3,2,1,0:T(8,128)(2,1)}, bf16[3,1,1,6,128,128]{4,5,3,2,1,0:T(8,128)(2,1)S(1)}, u32[]{:S(2)}) copy-start(bf16[3,1,1,6,128,128]{4,5,3,2,1,0:T(8,128)(2,1)S(1)} %collective-permute-done.9) | copy-start | bytes 1769476
  470.3 73.2 %collective-permute-start.10 = (bf16[3,3,1,6,128,128]{4,5,3,2,1,0:T(8,128)(2,1)}, bf16[3,3,1,6,128,128]{4,5,3,2,1,0:T(8,128)(2,1)}, u32[]{:S(2)}, u32[]{:S(2)}) collective-permute-start(bf16[3,3,1,6,128,128]{4,5,3,2,1,0:T(8,128)(2,1)} %pad_maximum_fusion.1), channel_id=1, source_target_pairs={{0,1},{2,3},{4,5},{6,7},{8,9},{10,11},{12,13},{14,15},{16,17},{18,... | collective-permute-start | bytes 5308424 | tf_op jit(solution)/shard_map/ppermute | solution.py:12
  472.8 75.0 %collective-permute-start.11 = (bf16[3,3,1,6,128,128]{4,5,3,2,1,0:T(8,128)(2,1)}, bf16[3,3,1,6,128,128]{4,5,3,2,1,0:T(8,128)(2,1)}, u32[]{:S(2)}, u32[]{:S(2)}) collective-permute-start(bf16[3,3,1,6,128,128]{4,5,3,2,1,0:T(8,128)(2,1)} %pad_maximum_fusion.1), channel_id=1, source_target_pairs={{1,0},{3,2},{5,4},{7,6},{9,8},{11,10},{13,12},{15,14},{17,16},{19,... | collective-permute-start | bytes 5308424 | tf_op jit(solution)/shard_map/ppermute | solution.py:15
  475.4 44.7 %copy-start.2 = (bf16[20,128,256]{1,2,0:T(8,128)(2,1)S(1)}, bf16[20,128,256]{1,2,0:T(8,128)(2,1)}, u32[]{:S(2)}) copy-start(bf16[20,128,256]{1,2,0:T(8,128)(2,1)} %get-tuple-element.237) | copy-start | bytes 3932164
where the time goes:
time: 561 us; the launch traced here: 555 us
  loops' own time  170 us (30%)
  local copies, waits for them, and re-layouts  103 us (18%)
  matrix products  89.1 us (16%)
  waiting for transfers between devices  64.4 us (11%)
  starting transfers between devices  56 us (10%)
  blocking collectives  40.4 us (7%)
  other arithmetic  32.2 us (6%)
    another operation x1, loops' own time, solve_local(): lax.scan(backward, empty, (store, diag_inverse, parent, places), reverse=...  99.9 us
    another operation x1, loops' own time, solve_local(): lax.scan(forward, store, (blocks[1:], diag_inverse[1:], coupling, parent[...  69.8 us
    ppermute x6, waiting for transfers between devices, with_halo(): lax.ppermute(lax.slice_in_dim(block, 0, width, axis=dim), axis, backward)  52.9 us
    ppermute x6, starting transfers between devices, with_halo(): lax.ppermute(lax.slice_in_dim(block, block.shape[dim] - width, None, axis...  48.3 us
    all_gather x1, blocking collectives, per_device(): lax.all_gather(coeffs, ('gx', 'gy', 'gz'), axis=1, tiled=True)  40.4 us
    dot_general x19, matrix products, forward(): jnp.einsum('rs,ts->rt', lower, inverse_blk, preferred_element_type=jnp.fl...  37 us
    scatter-add x6, other arithmetic, per_device(): total.at[:, send_rows[slot_id]].add(returned[slot_id].astype(jnp.float32))  26.3 us
    dynamic_slice x76, local copies, waits for them, and re-layouts, solve_local(): lax.scan(forward, store, (blocks[1:], diag_inverse[1:], coupling, parent[...  25.4 us
  transfers between devices with their start and end apart: 12, of which 7 were waited for; matrix products, arithmetic and copies ran while one was open for 7% of the time, Pallas kernels for 0%

commit v1 on v0

--- a/solution.py
+++ b/solution.py
@@ -2,6 +2,28 @@
 import jax.numpy as jnp
 from jax import lax
 from jax.sharding import PartitionSpec as P
+
+
+def joined_along(blocks, dim):
+    lengths = list(blocks.shape[1:])
+    lengths[dim] *= blocks.shape[0]
+    return jnp.moveaxis(blocks, 0, dim).reshape(lengths)
+
+
+def grow_blocks(x, axis):
+    count = lax.axis_size(axis)
+    tiles = x[None]
+    for level in range(count.bit_length() - 1):
+        bit = 1 << level
+        other = lax.ppermute(tiles, axis, [(i, i ^ bit) for i in range(count)])
+        both = jnp.stack([tiles, other])
+        upper = lax.axis_index(axis) >> level & 1
+        tiles = jnp.where(upper == 0, both, both[::-1]).reshape(-1, *x.shape)
+    return tiles
+
+
+def gather_by_bits(array, axis, dim):
+    return joined_along(grow_blocks(array, axis), dim)
 
 
 def with_halo(block, sides, width):
@@ -98,7 +120,7 @@
         returned.append(pick_slot(back, axis_pos, 0, 2 * axis_pos))
         returned.append(pick_slot(back, axis_pos, 2, 2 * axis_pos + 1))
     solved_coarse = lax.dot_general(
-        lax.all_gather(coeffs, ("gx", "gy", "gz"), axis=1, tiled=True),
+        gather_by_bits(coeffs, ("gx", "gy", "gz"), 1),
         coarse_inverse,
         (((1,), (1,)), ((), ())),
         precision=lax.Precision.HIGHEST,

time: 561 us -> 536 us (0.955)
  blocking collectives: 40.4 us -> 0 us
  starting transfers between devices: 56 us -> 71.2 us
  matrix products: 89.1 us -> 77 us
    all_gather x1 -> x0, blocking collectives: 40.4 us -> none  [per_device(): lax.all_gather(coeffs, ('gx', 'gy', 'gz'), axis=1, tiled=True)]
    ppermute x0 -> x5, starting transfers between devices: none -> 31.9 us  [grow_blocks(): other = lax.ppermute(tiles, axis, [(i, i ^ bit) for i in range(count)])]
    ppermute x0 -> x5, waiting for transfers between devices: none -> 26.3 us  [grow_blocks(): other = lax.ppermute(tiles, axis, [(i, i ^ bit) for i in range(count)])]
    ppermute x6, starting transfers between devices: 48.3 us -> 31.3 us  [with_halo(): lax.ppermute(lax.slice_in_dim(block, block.shape[dim] - width, None, axis...]
    dynamic_slice x76, local copies, waits for them, and re-layouts: 25.4 us -> 41.6 us  [solve_local(): lax.scan(forward, store, (blocks[1:], diag_inverse[1:], coupling, parent[...]
    dynamic_slice x19, local copies, waits for them, and re-layouts: 16.1 us -> 0.21 us  [forward(): prior = lax.dynamic_index_in_dim(store, link, 0, keepdims=False)]
    dot_general x19, matrix products: 37 us -> 24.9 us  [forward(): jnp.einsum('rs,ts->rt', lower, inverse_blk, preferred_element_type=jnp.fl...]
    ppermute x6, waiting for transfers between devices: 52.9 us -> 42.5 us  [with_halo(): lax.ppermute(lax.slice_in_dim(block, 0, width, axis=dim), axis, backward)]
  transfers between devices with their start and end apart: 12 -> 17, of which waited for: 7 -> 7; matrix products, arithmetic and copies ran while one was open for 7% -> 8% of each run, Pallas kernels for 0% -> 0%
where the time goes in v1:
time: 536 us; the launch traced here: 531 us
  loops' own time  171 us (32%)
  local copies, waits for them, and re-layouts  108 us (20%)
  matrix products  77 us (14%)
  starting transfers between devices  71.2 us (13%)
  waiting for transfers between devices  70 us (13%)
  other arithmetic  32.5 us (6%)
    another operation x1, loops' own time, solve_local(): lax.scan(backward, empty, (store, diag_inverse, parent, places), reverse=...  96.7 us
    another operation x1, loops' own time, solve_local(): lax.scan(forward, store, (blocks[1:], diag_inverse[1:], coupling, parent[...  74.7 us
    ppermute x6, waiting for transfers between devices, with_halo(): lax.ppermute(lax.slice_in_dim(block, 0, width, axis=dim), axis, backward)  42.5 us
    dynamic_slice x76, local copies, waits for them, and re-layouts, solve_local(): lax.scan(forward, store, (blocks[1:], diag_inverse[1:], coupling, parent[...  41.6 us
    ppermute x5, starting transfers between devices, grow_blocks(): other = lax.ppermute(tiles, axis, [(i, i ^ bit) for i in range(count)])  31.9 us
    ppermute x6, starting transfers between devices, with_halo(): lax.ppermute(lax.slice_in_dim(block, block.shape[dim] - width, None, axis...  31.3 us
    ppermute x5, waiting for transfers between devices, grow_blocks(): other = lax.ppermute(tiles, axis, [(i, i ^ bit) for i in range(count)])  26.3 us
    scatter-add x6, other arithmetic, per_device(): total.at[:, send_rows[slot_id]].add(returned[slot_id].astype(jnp.float32))  26.2 us
  transfers between devices with their start and end apart: 17, of which 7 were waited for; matrix products, arithmetic and copies ran while one was open for 8% of the time, Pallas kernels for 0%

profile of v1, /device:TPU:0, one launch (start us, length us, event | category | flops | bytes accessed | tf_op | source)
XLA Modules:
  0.0 530.7 jit_solution(482920418076629699)
XLA Ops:
  1.4 2.0 copy.16
  3.4 1.6 gather_fusion
  6.5 5.6 %collective-permute-start.1 = (f32[1,1,1,6,128,128]{4,5,3,2,1,0:T(8,128)S(1)}, f32[1,1,1,6,128,128]{4,5,3,2,1,0:T(8,128)S(1)}, u32[]{:S(2)}, u32[]{:S(2)}) collective-permute-start(f32[1,1,1,6,128,128]{4,5,3,2,1,0:T(8,128)S(1)} %select_bitcast_fusion), channel_id=1, source_target_pairs={{0,8},{8,16},{16,24},{1,9},{9,17},{17,25},{2,10},{10,18},{18,26},{... | collective-permute-start | bytes 1179656 | tf_op jit(solution)/shard_map/ppermute | solution.py:34
  12.1 7.2 %collective-permute-done = f32[1,1,1,6,128,128]{4,5,3,2,1,0:T(8,128)S(1)} collective-permute-done((f32[1,1,1,6,128,128]{4,5,3,2,1,0:T(8,128)S(1)}, f32[1,1,1,6,128,128]{4,5,3,2,1,0:T(8,128)S(1)}, u32[]{:S(2)}, u32[]{:S(2)}) %collective-permute-start) | collective-permute-done | bytes 393248 | tf_op jit(solution)/shard_map/ppermute | solution.py:37
  20.5 1.6 collective-permute-start.2
  22.1 4.6 collective-permute-start.3
  26.7 24.9 %collective-permute-done.2 = f32[3,1,1,6,128,128]{4,5,3,2,1,0:T(8,128)S(1)} collective-permute-done((f32[3,1,1,6,128,128]{4,5,3,2,1,0:T(8,128)S(1)}, f32[3,1,1,6,128,128]{4,5,3,2,1,0:T(8,128)S(1)}, u32[]{:S(2)}, u32[]{:S(2)}) %collective-permute-start.2) | collective-permute-done | bytes 1179680 | tf_op jit(solution)/shard_map/ppermute | solution.py:37
  51.6 2.3 pad_maximum_fusion
  55.5 6.7 %collective-permute-start.5 = (f32[3,3,1,6,128,128]{4,5,3,2,1,0:T(8,128)}, f32[3,3,1,6,128,128]{4,5,3,2,1,0:T(8,128)}, u32[]{:S(2)}, u32[]{:S(2)}) collective-permute-start(f32[3,3,1,6,128,128]{4,5,3,2,1,0:T(8,128)} %pad_maximum_fusion), channel_id=1, source_target_pairs={{0,1},{2,3},{4,5},{6,7},{8,9},{10,11},{12,13},{14,15},{16,17},{18,... | collective-permute-start | bytes 10616840 | tf_op jit(solution)/shard_map/ppermute | solution.py:34
  62.8 2.4 fusion.28
  65.3 1.5 constant_dynamic-update-slice_fusion.1
  66.8 3.5 slice.108
  74.7 1.7 slice.133
  77.6 141.3 %while.28 = (s32[]{:T(128)}, bf16[20,128,256]{2,1,0:T(8,128)(2,1)S(1)}, f32[19,128,256]{1,2,0:T(8,128)}, s32[19]{0:T(128)S(1)}, bf16[19,256,256]{2,1,0:T(8,128)(...) while((s32[]{:T(128)}, ...), condition=%wide.region_1.2_spmd, body=%wide.region_0.1_spmd.sunk | while | flops 33652744 | bytes 1180877 | solution.py:66
  83.7 1.3 fusion.75
  91.2 1.3 fusion.75
  98.6 1.3 fusion.75
  113.5 1.3 fusion.75
  128.4 1.3 fusion.75
  150.7 1.3 fusion.75
  165.6 1.3 fusion.75
  187.9 1.3 fusion.75
  202.8 1.3 fusion.75
  220.3 1.4 broadcast.135.clone
  221.7 179.9 %while.29 = (s32[]{:T(128)}, f32[20,128,256]{2,1,0:T(8,128)S(1)}, bf16[20,128,256]{1,2,0:T(8,128)(2,1)}, s32[20]{0:T(128)S(1)}, bf16[20,128,256]{2,1,0:T(8,128)(...) while((s32[]{:T(128)}, f32[20,128,256]{2,1,0:T(8,128)S(1)}, ...), condition=%wide.region_3.4_spmd, body=%wide.region_2.3_spmd.sunk | while | flops 33751048 | bytes 1378079 | solution.py:87
  402.5 4.4 collective-permute-start.11
  408.2 22.4 %collective-permute-start.7 = (f32[2,128,40]{1,2,0:T(8,128)S(1)}, f32[2,128,40]{1,2,0:T(8,128)S(1)}, u32[]{:S(2)}, u32[]{:S(2)}) collective-permute-start(f32[2,128,40]{1,2,0:T(8,128)S(1)} %get-tuple-element.276), channel_id=1, source_target_pairs={{0,2},{1,3},{2,0},{3,1},{4,6},{5,7},{6,4},{7,5},{8,10},{9,11},{10,... | collective-permute-start | bytes 122888 | tf_op jit(solution)/shard_map/ppermute | solution.py:18
  430.6 2.0 collective-permute-done.7
  432.7 7.4 %collective-permute-start.13 = (bf16[3,1,1,6,128,128]{4,5,3,2,1,0:T(8,128)(2,1)S(1)}, bf16[3,1,1,6,128,128]{4,5,3,2,1,0:T(8,128)(2,1)S(1)}, u32[]{:S(2)}, u32[]{:S(2)}) collective-permute-start(bf16[3,1,1,6,128,128]{4,5,3,2,1,0:T(8,128)(2,1)S(1)} %pad_maximum_fusion.4), channel_id=1, source_target_pairs={{0,2},{2,4},{4,6},{1,3},{3,5},{5,7},{8,10},{10,12},{12,14},{9,11},... | collective-permute-start | bytes 1769480 | tf_op jit(solution)/shard_map/ppermute | solution.py:34
  441.5 5.5 %collective-permute-start.8 = (f32[4,128,40]{1,2,0:T(8,128)S(1)}, f32[4,128,40]{1,2,0:T(8,128)S(1)}, u32[]{:S(2)}, u32[]{:S(2)}) collective-permute-start(f32[4,128,40]{1,2,0:T(8,128)S(1)} %bitcast.248), channel_id=1, source_target_pairs={{0,4},{1,5},{2,6},{3,7},{4,0},{5,1},{6,2},{7,3},{8,12},{9,13},{10,... | collective-permute-start | bytes 245768 | tf_op jit(solution)/shard_map/ppermute | solution.py:18
  447.0 9.8 %collective-permute-done.8 = f32[4,128,40]{1,2,0:T(8,128)S(1)} collective-permute-done((f32[4,128,40]{1,2,0:T(8,128)S(1)}, f32[4,128,40]{1,2,0:T(8,128)S(1)}, u32[]{:S(2)}, u32[]{:S(2)}) %collective-permute-start.8) | collective-permute-done | bytes 81952 | tf_op jit(solution)/shard_map/ppermute | solution.py:18
  456.8 1.5 collective-permute-start.9
  458.3 10.5 %collective-permute-done.14 = bf16[3,1,1,6,128,128]{4,5,3,2,1,0:T(8,128)(2,1)S(1)} collective-permute-done((bf16[3,1,1,6,128,128]{4,5,3,2,1,0:T(8,128)(2,1)S(1)}, bf16[3,1,1,6,128,128]{4,5,3,2,1,0:T(8,128)(2,1)S(1)}, u32[]{:S(2)}, u32[]{:S(2)}) %collective-permute-start.14) | collective-permute-done | bytes 589856 | tf_op jit(solution)/shard_map/ppermute | solution.py:37
  468.8 1.4 pad_maximum_fusion.1
  470.2 2.5 collective-permute-start.15
  474.1 2.5 collective-permute-start.10
  477.2 14.5 %collective-permute-done.10 = f32[16,128,40]{1,2,0:T(8,128)S(1)} collective-permute-done((f32[16,128,40]{1,2,0:T(8,128)S(1)}, f32[16,128,40]{1,2,0:T(8,128)S(1)}, u32[]{:S(2)}, u32[]{:S(2)}) %collective-permute-start.10) | collective-permute-done | bytes 327712 | tf_op jit(solution)/shard_map/ppermute | solution.py:18
  491.8 1.8 fusion.57
  494.8 1.7 copy.25
  496.4 3.1 convolution_add_fusion
  499.6 1.9 copy.20
  501.5 4.4 scatter_custom_fusion
  505.9 4.4 scatter_custom_fusion.1
  510.2 4.4 scatter_custom_fusion.2
  514.6 4.4 scatter_custom_fusion.3
  519.0 4.4 scatter_custom_fusion.4
  523.4 4.4 scatter_custom_fusion.5
  527.7 3.0 copy.21
  (325 shorter events, 157.6 us)
Async XLA Ops:
  0.0 491.8 %copy-start = (f32[40,1280]{1,0:T(8,128)S(1)}, f32[40,1280]{1,0:T(8,128)}, u32[]{:S(2)}) copy-start(f32[40,1280]{1,0:T(8,128)} %param.21) | copy-start | bytes 614404
  5.2 14.0 %collective-permute-start = (f32[1,1,1,6,128,128]{4,5,3,2,1,0:T(8,128)S(1)}, f32[1,1,1,6,128,128]{4,5,3,2,1,0:T(8,128)S(1)}, u32[]{:S(2)}, u32[]{:S(2)}) collective-permute-start(f32[1,1,1,6,128,128]{4,5,3,2,1,0:T(8,128)S(1)} %select_bitcast_fusion), channel_id=1, source_target_pairs={{8,0},{16,8},{24,16},{9,1},{17,9},{25,17},{10,2},{18,10},{26,18},{... | collective-permute-start | bytes 1179656 | tf_op jit(solution)/shard_map/ppermute | solution.py:37
  6.5 13.9 %collective-permute-start.1 = (f32[1,1,1,6,128,128]{4,5,3,2,1,0:T(8,128)S(1)}, f32[1,1,1,6,128,128]{4,5,3,2,1,0:T(8,128)S(1)}, u32[]{:S(2)}, u32[]{:S(2)}) collective-permute-start(f32[1,1,1,6,128,128]{4,5,3,2,1,0:T(8,128)S(1)} %select_bitcast_fusion), channel_id=1, source_target_pairs={{0,8},{8,16},{16,24},{1,9},{9,17},{17,25},{2,10},{10,18},{18,26},{... | collective-permute-start | bytes 1179656 | tf_op jit(solution)/shard_map/ppermute | solution.py:34
  20.4 33.5 %copy-start.6 = (f32[1,1,1,6,128,128]{4,5,3,2,1,0:T(8,128)}, f32[1,1,1,6,128,128]{4,5,3,2,1,0:T(8,128)S(1)}, u32[]{:S(2)}) copy-start(f32[1,1,1,6,128,128]{4,5,3,2,1,0:T(8,128)S(1)} %collective-permute-done.1) | copy-start | bytes 1179652
  20.5 42.3 %copy-start.2 = (f32[128,4352]{1,0:T(8,128)S(1)}, f32[128,4352]{1,0:T(8,128)}, u32[]{:S(2)}) copy-start(f32[128,4352]{1,0:T(8,128)} %param.14) | copy-start | bytes 6684676
  20.5 42.3 %copy-start.5 = (f32[40,4352]{1,0:T(8,128)S(1)}, f32[40,4352]{1,0:T(8,128)}, u32[]{:S(2)}) copy-start(f32[40,4352]{1,0:T(8,128)} %param.20) | copy-start | bytes 2088964
  20.5 31.1 %collective-permute-start.2 = (f32[3,1,1,6,128,128]{4,5,3,2,1,0:T(8,128)S(1)}, f32[3,1,1,6,128,128]{4,5,3,2,1,0:T(8,128)S(1)}, u32[]{:S(2)}, u32[]{:S(2)}) collective-permute-start(f32[3,1,1,6,128,128]{4,5,3,2,1,0:T(8,128)S(1)} %pad_maximum_fusion.2), channel_id=1, source_target_pairs={{2,0},{4,2},{6,4},{3,1},{5,3},{7,5},{10,8},{12,10},{14,12},{11,9},... | collective-permute-start | bytes 3538952 | tf_op jit(solution)/shard_map/ppermute | solution.py:37
  22.1 29.5 %collective-permute-start.3 = (f32[3,1,1,6,128,128]{4,5,3,2,1,0:T(8,128)S(1)}, f32[3,1,1,6,128,128]{4,5,3,2,1,0:T(8,128)S(1)}, u32[]{:S(2)}, u32[]{:S(2)}) collective-permute-start(f32[3,1,1,6,128,128]{4,5,3,2,1,0:T(8,128)S(1)} %pad_maximum_fusion.2), channel_id=1, source_target_pairs={{0,2},{2,4},{4,6},{1,3},{3,5},{5,7},{8,10},{10,12},{12,14},{9,11},... | collective-permute-start | bytes 3538952 | tf_op jit(solution)/shard_map/ppermute | solution.py:34
  51.6 2.3 copy-start.7
  51.6 2.6 copy-start.8
  54.2 18.9 %collective-permute-start.4 = (f32[3,3,1,6,128,128]{4,5,3,2,1,0:T(8,128)}, f32[3,3,1,6,128,128]{4,5,3,2,1,0:T(8,128)}, u32[]{:S(2)}, u32[]{:S(2)}) collective-permute-start(f32[3,3,1,6,128,128]{4,5,3,2,1,0:T(8,128)} %pad_maximum_fusion), channel_id=1, source_target_pairs={{1,0},{3,2},{5,4},{7,6},{9,8},{11,10},{13,12},{15,14},{17,16},{19,... | collective-permute-start | bytes 10616840 | tf_op jit(solution)/shard_map/ppermute | solution.py:37
  55.5 18.4 %collective-permute-start.5 = (f32[3,3,1,6,128,128]{4,5,3,2,1,0:T(8,128)}, f32[3,3,1,6,128,128]{4,5,3,2,1,0:T(8,128)}, u32[]{:S(2)}, u32[]{:S(2)}) collective-permute-start(f32[3,3,1,6,128,128]{4,5,3,2,1,0:T(8,128)} %pad_maximum_fusion), channel_id=1, source_target_pairs={{0,1},{2,3},{4,5},{6,7},{8,9},{10,11},{12,13},{14,15},{16,17},{18,... | collective-permute-start | bytes 10616840 | tf_op jit(solution)/shard_map/ppermute | solution.py:34
  65.2 5.3 collective-permute-start.6
  66.8 3.6 copy-start.14
  66.8 3.7 copy-start.1
  219.0 1.1 copy-start.4
  402.5 30.1 %collective-permute-start.11 = (bf16[1,1,1,6,128,128]{4,5,3,2,1,0:T(8,128)(2,1)S(1)}, bf16[1,1,1,6,128,128]{4,5,3,2,1,0:T(8,128)(2,1)S(1)}, u32[]{:S(2)}, u32[]{:S(2)}) collective-permute-start(bf16[1,1,1,6,128,128]{4,5,3,2,1,0:T(8,128)(2,1)S(1)} %bitcast.239), channel_id=1, source_target_pairs={{0,8},{8,16},{16,24},{1,9},{9,17},{17,25},{2,10},{10,18},{18,26},{... | collective-permute-start | bytes 589832 | tf_op jit(solution)/shard_map/ppermute | solution.py:34
  406.9 25.7 %collective-permute-start.12 = (bf16[1,1,1,6,128,128]{4,5,3,2,1,0:T(8,128)(2,1)S(1)}, bf16[1,1,1,6,128,128]{4,5,3,2,1,0:T(8,128)(2,1)S(1)}, u32[]{:S(2)}, u32[]{:S(2)}) collective-permute-start(bf16[1,1,1,6,128,128]{4,5,3,2,1,0:T(8,128)(2,1)S(1)} %bitcast.240), channel_id=1, source_target_pairs={{8,0},{16,8},{24,16},{9,1},{17,9},{25,17},{10,2},{18,10},{26,18},{... | collective-permute-start | bytes 589832 | tf_op jit(solution)/shard_map/ppermute | solution.py:37
  408.2 24.4 %collective-permute-start.7 = (f32[2,128,40]{1,2,0:T(8,128)S(1)}, f32[2,128,40]{1,2,0:T(8,128)S(1)}, u32[]{:S(2)}, u32[]{:S(2)}) collective-permute-start(f32[2,128,40]{1,2,0:T(8,128)S(1)} %get-tuple-element.276), channel_id=1, source_target_pairs={{0,2},{1,3},{2,0},{3,1},{4,6},{5,7},{6,4},{7,5},{8,10},{9,11},{10,... | collective-permute-start | bytes 122888 | tf_op jit(solution)/shard_map/ppermute | solution.py:18
  432.6 37.6 %copy-start.9 = (bf16[1,1,1,6,128,128]{4,5,3,2,1,0:T(8,128)(2,1)}, bf16[1,1,1,6,128,128]{4,5,3,2,1,0:T(8,128)(2,1)S(1)}, u32[]{:S(2)}) copy-start(bf16[1,1,1,6,128,128]{4,5,3,2,1,0:T(8,128)(2,1)S(1)} %collective-permute-done.11) | copy-start | bytes 589828
  432.6 37.6 %copy-start.10 = (bf16[1,1,1,6,128,128]{4,5,3,2,1,0:T(8,128)(2,1)}, bf16[1,1,1,6,128,128]{4,5,3,2,1,0:T(8,128)(2,1)S(1)}, u32[]{:S(2)}) copy-start(bf16[1,1,1,6,128,128]{4,5,3,2,1,0:T(8,128)(2,1)S(1)} %collective-permute-done.12) | copy-start | bytes 589828
  432.7 25.6 %collective-permute-start.13 = (bf16[3,1,1,6,128,128]{4,5,3,2,1,0:T(8,128)(2,1)S(1)}, bf16[3,1,1,6,128,128]{4,5,3,2,1,0:T(8,128)(2,1)S(1)}, u32[]{:S(2)}, u32[]{:S(2)}) collective-permute-start(bf16[3,1,1,6,128,128]{4,5,3,2,1,0:T(8,128)(2,1)S(1)} %pad_maximum_fusion.4), channel_id=1, source_target_pairs={{0,2},{2,4},{4,6},{1,3},{3,5},{5,7},{8,10},{10,12},{12,14},{9,11},... | collective-permute-start | bytes 1769480 | tf_op jit(solution)/shard_map/ppermute | solution.py:34
  440.2 28.6 %collective-permute-start.14 = (bf16[3,1,1,6,128,128]{4,5,3,2,1,0:T(8,128)(2,1)S(1)}, bf16[3,1,1,6,128,128]{4,5,3,2,1,0:T(8,128)(2,1)S(1)}, u32[]{:S(2)}, u32[]{:S(2)}) collective-permute-start(bf16[3,1,1,6,128,128]{4,5,3,2,1,0:T(8,128)(2,1)S(1)} %pad_maximum_fusion.4), channel_id=1, source_target_pairs={{2,0},{4,2},{6,4},{3,1},{5,3},{7,5},{10,8},{12,10},{14,12},{11,9},... | collective-permute-start | bytes 1769480 | tf_op jit(solution)/shard_map/ppermute | solution.py:37
  441.5 15.3 %collective-permute-start.8 = (f32[4,128,40]{1,2,0:T(8,128)S(1)}, f32[4,128,40]{1,2,0:T(8,128)S(1)}, u32[]{:S(2)}, u32[]{:S(2)}) collective-permute-start(f32[4,128,40]{1,2,0:T(8,128)S(1)} %bitcast.248), channel_id=1, source_target_pairs={{0,4},{1,5},{2,6},{3,7},{4,0},{5,1},{6,2},{7,3},{8,12},{9,13},{10,... | collective-permute-start | bytes 245768 | tf_op jit(solution)/shard_map/ppermute | solution.py:18
  456.8 19.8 %copy-start.13 = (s32[6,128]{1,0:T(8,128)S(1)}, s32[6,128]{1,0:T(8,128)}, u32[]{:S(2)}) copy-start(s32[6,128]{1,0:T(8,128)} %param.18) | copy-start | bytes 9220
  456.8 17.2 %collective-permute-start.9 = (f32[8,128,40]{1,2,0:T(8,128)S(1)}, f32[8,128,40]{1,2,0:T(8,128)S(1)}, u32[]{:S(2)}, u32[]{:S(2)}) collective-permute-start(f32[8,128,40]{1,2,0:T(8,128)S(1)} %bitcast.245), channel_id=1, source_target_pairs={{0,8},{1,9},{2,10},{3,11},{4,12},{5,13},{6,14},{7,15},{8,0},{9,1},... | collective-permute-start | bytes 491528 | tf_op jit(solution)/shard_map/ppermute | solution.py:18
  458.3 15.8 %copy-start.11 = (bf16[3,1,1,6,128,128]{4,5,3,2,1,0:T(8,128)(2,1)}, bf16[3,1,1,6,128,128]{4,5,3,2,1,0:T(8,128)(2,1)S(1)}, u32[]{:S(2)}) copy-start(bf16[3,1,1,6,128,128]{4,5,3,2,1,0:T(8,128)(2,1)S(1)} %collective-permute-done.13) | copy-start | bytes 1769476
  468.8 5.3 copy-start.12
  470.2 48.8 %collective-permute-start.15 = (bf16[3,3,1,6,128,128]{4,5,3,2,1,0:T(8,128)(2,1)}, bf16[3,3,1,6,128,128]{4,5,3,2,1,0:T(8,128)(2,1)}, u32[]{:S(2)}, u32[]{:S(2)}) collective-permute-start(bf16[3,3,1,6,128,128]{4,5,3,2,1,0:T(8,128)(2,1)} %pad_maximum_fusion.1), channel_id=1, source_target_pairs={{0,1},{2,3},{4,5},{6,7},{8,9},{10,11},{12,13},{14,15},{16,17},{18,... | collective-permute-start | bytes 5308424 | tf_op jit(solution)/shard_map/ppermute | solution.py:34
  472.7 50.6 %collective-permute-start.16 = (bf16[3,3,1,6,128,128]{4,5,3,2,1,0:T(8,128)(2,1)}, bf16[3,3,1,6,128,128]{4,5,3,2,1,0:T(8,128)(2,1)}, u32[]{:S(2)}, u32[]{:S(2)}) collective-permute-start(bf16[3,3,1,6,128,128]{4,5,3,2,1,0:T(8,128)(2,1)} %pad_maximum_fusion.1), channel_id=1, source_target_pairs={{1,0},{3,2},{5,4},{7,6},{9,8},{11,10},{13,12},{15,14},{17,16},{19,... | collective-permute-start | bytes 5308424 | tf_op jit(solution)/shard_map/ppermute | solution.py:37
  474.1 19.6 %copy-start.3 = (bf16[20,128,256]{1,2,0:T(8,128)(2,1)S(1)}, bf16[20,128,256]{1,2,0:T(8,128)(2,1)}, u32[]{:S(2)}) copy-start(bf16[20,128,256]{1,2,0:T(8,128)(2,1)} %get-tuple-element.237) | copy-start | bytes 3932164
  474.1 17.6 %collective-permute-start.10 = (f32[16,128,40]{1,2,0:T(8,128)S(1)}, f32[16,128,40]{1,2,0:T(8,128)S(1)}, u32[]{:S(2)}, u32[]{:S(2)}) collective-permute-start(f32[16,128,40]{1,2,0:T(8,128)S(1)} %bitcast.243), channel_id=1, source_target_pairs={{0,16},{1,17},{2,18},{3,19},{4,20},{5,21},{6,22},{7,23},{8,24},{9,... | collective-permute-start | bytes 983048 | tf_op jit(solution)/shard_map/ppermute | solution.py:18
